TPU v7x, 256 devices: a whole 4x4x8 slice. The times are simulated.
256 devices in a mesh: grp: 8 (over x, core), dev: 32 (over z, y).
Axes of the slice: x: 4, y: 4, z: 8, core: 2. Of those that a mesh axis runs over, the one named last changes fastest.
Arguments:
- references: bfloat16 [192, 2048], P('dev'), may hold values from -4 to 4
- particles: bfloat16 [2048, 65536], P(None, ('grp', 'dev')), may hold values from -1300 to 1300
- defocus_bin: int32 [65536], P(('grp', 'dev')), may hold values from 0 to 63
- contrast_table: float32 [64, 32], replicated, may hold values from 0.1 to 1
- noise_power: float32 [32], replicated, may hold values from 300 to 3000
- class_prior: float32 [192], replicated, may hold values from -3 to 3
Outputs:
- new_references: float32 [192, 2048], P('dev')
- occupancy: float32 [192], P('dev')
All inputs are finite; a program needn't handle non-finite values.
Results may differ from a plain program's by a relative error of at most 0.0015.
Values may be sent and summed in bfloat16 or wider, within the bound.
No kernel may reach another device: no remote copies, remote signals or barrier semaphores. Data moves between devices by JAX's collectives and lax.ppermute only.
A program may use at most 64 MiB of HBM per device.

v0:
```python
import math
import jax
import jax.numpy as jnp
from jax import lax
from jax.sharding import PartitionSpec as P

Q = 32
M = 32
R = 128
CLS_DEV = 6


def angle_tables(cycle_freqs, count_turns):
    freq_index = jnp.arange(cycle_freqs, dtype=jnp.int32)
    turn_index = jnp.arange(count_turns, dtype=jnp.int32)
    wrapped = freq_index[:, None] * turn_index[None, :] % count_turns
    phases = 2.0 * math.pi / count_turns * wrapped.astype(jnp.float32)
    factor = jnp.where(freq_index == 0, 1.0, 2.0).astype(jnp.float32)[:, None]
    cosine = jnp.cos(phases)
    sine_part = jnp.sin(phases)
    score_table = jnp.stack([factor * cosine, factor * sine_part], 0).astype(jnp.bfloat16)
    turn_table = jnp.stack([cosine, sine_part], 0).astype(jnp.bfloat16)
    return (score_table, turn_table)


def particle_terms(particles, defocus_bin, contrast_table, noise_power):
    columns = particles.shape[1]
    cycle_count = contrast_table.shape[1]
    freq_count = particles.shape[0] // (2 * cycle_count)
    onehot = (
        defocus_bin[None, :] == jnp.arange(contrast_table.shape[0], dtype=jnp.int32)[:, None]
    ).astype(jnp.float32)
    contrast = jnp.dot(contrast_table.T, onehot, precision=lax.Precision.HIGHEST)
    scaled = contrast / noise_power[:, None]
    power_term = contrast * scaled
    weighted = (
        particles.astype(jnp.float32).reshape(freq_count, 2, cycle_count, columns)
        * scaled[None, None]
    ).astype(jnp.bfloat16)
    return (weighted.reshape(freq_count, 2 * cycle_count, columns), power_term)


def class_rows(class_block):
    classes = class_block.shape[0]
    class_grid = class_block.reshape(classes, M, 2, Q)
    real_part = class_grid[:, :, 0, :]
    imag_part = class_grid[:, :, 1, :]
    rows_real = jnp.concatenate([real_part, imag_part], -1)
    rows_imag = jnp.concatenate([-imag_part, real_part], -1)
    stacked = jnp.stack([rows_real, rows_imag], 0)
    factor = jnp.where(jnp.arange(M) == 0, 1.0, 2.0).astype(jnp.float32)
    squares = class_grid.astype(jnp.float32) ** 2
    cycle_power = jnp.sum(jnp.sum(squares, axis=2) * factor[None, :, None], axis=1)
    return (stacked, cycle_power)


def block_rows(total_rows):
    return CLS_DEV * math.gcd(total_rows // CLS_DEV, 4)


def local(references, particles, defocus_bin, contrast_table, noise_power, class_prior):
    weighted, power_term = particle_terms(particles, defocus_bin, contrast_table, noise_power)
    score_table, turn_table = angle_tables(M, R)
    columns = particles.shape[1]
    classes_total = CLS_DEV * lax.axis_size("dev")

    def block_scores(class_block, first_row):
        stacked, cycle_power = class_rows(class_block)
        prior_part = lax.dynamic_slice_in_dim(class_prior, first_row, class_block.shape[0], 0)
        crossed = jnp.einsum(
            "pkmc,mcb->pmkb", stacked, weighted, preferred_element_type=jnp.float32
        ).astype(jnp.bfloat16)
        scores = jnp.einsum(
            "pmkb,pmr->krb", crossed, score_table, preferred_element_type=jnp.float32
        )
        penalty = jnp.dot(cycle_power, power_term, precision=lax.Precision.HIGHEST)
        return scores - 0.5 * penalty[:, None, :] + prior_part[:, None, None]

    initial = (jnp.full((columns,), -1e30, jnp.float32), jnp.zeros((columns,), jnp.float32))
    empty_sums = (
        jnp.zeros((classes_total, 2 * M * Q), jnp.float32),
        jnp.zeros((classes_total, Q), jnp.float32),
        jnp.zeros((classes_total,), jnp.float32),
    )
    gathered = lax.all_gather(references, "dev", axis=0, tiled=True)
    height = block_rows(gathered.shape[0])
    block_count = gathered.shape[0] // height
    blocks = gathered.reshape(block_count, height, gathered.shape[1])

    def one_block(current, block_item):
        class_block, offset = block_item
        scores = block_scores(class_block, offset * height)
        block_max = jnp.max(scores, axis=(0, 1))
        new_max = jnp.maximum(current[0], block_max)
        block_total = jnp.sum(jnp.exp(scores - new_max[None, None, :]), axis=(0, 1))
        return ((new_max, current[1] * jnp.exp(current[0] - new_max) + block_total), None)

    result, unused = lax.scan(
        one_block, initial, (blocks, jnp.arange(block_count, dtype=jnp.int32))
    )
    log_norm = result[0] + jnp.log(result[1])
    add_height = block_rows(gathered.shape[0])
    block_count = gathered.shape[0] // add_height
    blocks = gathered.reshape(block_count, add_height, gathered.shape[1])

    def one_block(current, block_item):
        class_block, offset = block_item
        row_start = offset * add_height
        scores = block_scores(class_block, row_start)
        responsibility = jnp.exp(scores - log_norm[None, None, :]).astype(jnp.bfloat16)
        spectra = jnp.einsum(
            "krb,pmr->pmkb", responsibility, turn_table, preferred_element_type=jnp.float32
        ).astype(jnp.bfloat16)
        products = jnp.einsum(
            "pmkb,mcb->kpmc", spectra, weighted, preferred_element_type=jnp.float32
        )
        real_sum = products[:, 0, :, :Q] + products[:, 1, :, Q:]
        imag_sum = products[:, 0, :, Q:] - products[:, 1, :, :Q]
        numerator = jnp.stack([real_sum, imag_sum], 2).reshape(add_height, 2 * M * Q)
        class_weight = jnp.sum(responsibility.astype(jnp.float32), axis=1)
        cycle_sum = jnp.dot(class_weight, power_term.T, precision=lax.Precision.HIGHEST)
        class_mass = jnp.sum(class_weight, axis=1)
        updated = (
            lax.dynamic_update_slice_in_dim(current[0], numerator, row_start, 0),
            lax.dynamic_update_slice_in_dim(current[1], cycle_sum, row_start, 0),
            lax.dynamic_update_slice_in_dim(current[2], class_mass, row_start, 0),
        )
        return (updated, None)

    result, unused = lax.scan(
        one_block, empty_sums, (blocks, jnp.arange(block_count, dtype=jnp.int32))
    )
    numer_all, cycles_all, mass_all = result
    merged = lax.psum((numer_all, cycles_all, mass_all), ("grp", "dev"))
    own_start = lax.axis_index("dev") * CLS_DEV
    numerator = lax.dynamic_slice_in_dim(merged[0], own_start, CLS_DEV, 0)
    cycle_sum = lax.dynamic_slice_in_dim(merged[1], own_start, CLS_DEV, 0)
    class_mass = lax.dynamic_slice_in_dim(merged[2], own_start, CLS_DEV, 0)
    new_references = (numerator.reshape(CLS_DEV, M, 2, Q) / cycle_sum[:, None, None, :]).reshape(
        CLS_DEV, 2 * M * Q
    )
    particle_total = columns * lax.axis_size("grp") * lax.axis_size("dev")
    occupancy = class_mass * (classes_total / particle_total)
    return (new_references, occupancy)


def solution(mesh):
    return jax.shard_map(
        local,
        mesh=mesh,
        in_specs=(P("dev", None), P(None, ("grp", "dev")), P(("grp", "dev")), P(), P(), P()),
        out_specs=(P("dev", None), P("dev")),
        check_vma=False,
    )
```

profile of v0, /device:TPU:2, one launch (start us, length us, event | category | flops | bytes accessed | tf_op | source)
XLA Modules:
  0.0 525.7 jit_solution(9444845568496355798)
XLA Ops:
  7.5 53.8 %all-gather = bf16[32,6,2048]{2,1,0:T(8,128)(2,1)S(1)} all-gather(bf16[1,6,2048]{2,1,0:T(8,128)(2,1)} %bitcast.179), channel_id=1, replica_groups=mesh['grp'=8,'dev'=32] {'dev'}, dimensions={0}, use_global_device_ids=true | all-gather | bytes 811008 | tf_op jit(solution)/shard_map/all_gather | solution.py:85
  64.5 87.8 %while.28 = (s32[]{:T(128)}, f32[256]{0:T(256)S(1)}, f32[256]{0:T(256)S(1)}, bf16[8,24,2048]{2,1,0:T(8,128)(2,1)}, bf16[32,64,256]{2,1,0:T(8,128)(2,1)}, /*index...) while((s32[]{:T(128)}, f32[256]{0:T(256)S(1)}, ...), condition=%wide.region_5.6_spmd.clone, body=%wide.region_0.5_spmd.clone.sunk | while | flops 159947328 | bytes 10727242 | solution.py:98
  67.3 2.5 fusion.111
  72.5 2.0 fusion.112
  78.3 2.5 fusion.111
  83.5 2.0 fusion.112
  89.2 2.5 fusion.111
  94.5 2.0 fusion.112
  100.2 2.5 fusion.111
  105.5 2.0 fusion.112
  111.2 2.5 fusion.111
  116.5 2.0 fusion.112
  122.2 2.5 fusion.111
  127.4 2.0 fusion.112
  133.2 2.5 fusion.111
  138.4 2.0 fusion.112
  144.2 2.5 fusion.111
  149.4 2.0 fusion.112
  152.6 106.6 %while.27 = (s32[]{:T(128)}, f32[192,2048]{1,0:T(8,128)S(1)}, f32[192,32]{1,0:T(8,128)S(1)}, f32[192]{0:T(256)S(1)}, bf16[8,24,2048]{2,1,0:T(8,128)(2,1)}, /*ind...) while((s32[]{:T(128)}, f32[192,2048]{1,0:T(8,128)S(1)}, ...), condition=%wide.region_11.12_spmd, body=%wide.region_6.11_spmd.sunk | while | flops 313785664 | bytes 12832803 | solution.py:130
  161.6 2.0 convolution_bitcast_fusion.3
  188.2 2.0 convolution_bitcast_fusion.3
  201.5 2.0 convolution_bitcast_fusion.3
  260.4 73.8 %all-reduce = (f32[192,32]{1,0:T(8,128)S(1)}, f32[192]{0:T(256)S(1)}) all-reduce(f32[192,32]{1,0:T(8,128)S(1)} %get-tuple-element.117, f32[192]{0:T(256)S(1)} %get-tuple-element.118), channel_id=1, replica_groups=mesh['grp'=8,'dev'=32] {'grp','dev'}, use_global_device_ids=true, to_apply=%region_13.14 | all-reduce | flops 6336 | bytes 50688 | tf_op jit(solution)/shard_map/psum | solution.py:134
  335.1 182.2 %all-reduce.3.cloned.1.call-done = f32[192,2048]{1,0:T(8,128)} async-done(((f32[192,2048]{1,0:T(8,128)}), f32[192,2048]{1,0:T(8,128)}) %all-reduce.3.cloned.1.call-update) | async-done | bytes 1572880 | tf_op jit(solution)/shard_map/psum | solution.py:134
  (349 shorter events, 147.8 us)
Async XLA Ops:
  7.2 55.2 %copy-start = (f32[64,32]{0,1:T(8,128)S(1)}, f32[64,32]{0,1:T(8,128)}, u32[]{:S(2)}) copy-start(f32[64,32]{0,1:T(8,128)} %param.13) | copy-start | bytes 24580
  7.2 56.1 %copy-start.2 = (bf16[2048,256]{1,0:T(8,128)(2,1)S(1)}, bf16[2048,256]{1,0:T(8,128)(2,1)}, u32[]{:S(2)}) copy-start(bf16[2048,256]{1,0:T(8,128)(2,1)} %param.11) | copy-start | bytes 3145732
  7.2 57.3 %copy-start.3 = (f32[192]{0:T(256)S(1)}, f32[192]{0:T(256)}, u32[]{:S(2)}) copy-start(f32[192]{0:T(256)} %param.15) | copy-start | bytes 2308
  7.2 510.1 %all-reduce.3.cloned.1.call-start = ((), (), s32[]{:S(2)}) async-start(), calls=%async_computation | async-start | bytes 3145728 | tf_op jit(solution)/shard_map/psum | solution.py:134
  259.2 1.1 copy-start.1
Sparse Core Ops, SparseCore 0:
  260.5 256.7 all-reduce.2
where the time goes:
time: 528 us; the launch traced here: 526 us
  waiting for transfers between devices  182 us (34%)
  blocking collectives  128 us (24%)
  matrix products  82.1 us (16%)
  local copies, waits for them, and re-layouts  64.7 us (12%)
  other arithmetic  42.8 us (8%)
  between operations  14.2 us (3%)
  loops' own time  12.1 us (2%)
    psum x1, waiting for transfers between devices, local(): merged = lax.psum((numer_all, cycles_all, mass_all), ('grp', 'dev'))  182 us
    psum x1, blocking collectives, local(): merged = lax.psum((numer_all, cycles_all, mass_all), ('grp', 'dev'))  73.8 us
    all_gather x1, blocking collectives, local(): gathered = lax.all_gather(references, 'dev', axis=0, tiled=True)  53.8 us
    dot_general x16, matrix products, block_scores(): jnp.einsum('pkmc,mcb->pmkb', stacked, weighted, preferred_element_type=jn...  32.7 us
    dot_general x16, matrix products, block_scores(): jnp.einsum('pmkb,pmr->krb', crossed, score_table, preferred_element_type=...  26.3 us
    dynamic_slice x32, local copies, waits for them, and re-layouts, local(): lax.scan(one_block, initial, (blocks, jnp.arange(block_count, dtype=jnp.i...  23.9 us
    reduce_sum x16, other arithmetic, class_rows(): jnp.sum(squares, axis=2) * factor[None, :, None]  18.6 us
    dot_general x8, matrix products, one_block(): jnp.einsum('pmkb,mcb->kpmc', spectra, weighted, preferred_element_type=jn...  15.7 us
  transfers between devices with their start and end apart: 1, of which 1 were waited for; matrix products, arithmetic and copies ran while one was open for 0% of the time, Pallas kernels for 0%

commit v1 on v0

--- a/solution.py
+++ b/solution.py
@@ -82,7 +82,9 @@
         jnp.zeros((classes_total, Q), jnp.float32),
         jnp.zeros((classes_total,), jnp.float32),
     )
-    gathered = lax.all_gather(references, "dev", axis=0, tiled=True)
+    gathered = jnp.concatenate(
+        lax.all_to_all(jnp.stack([references] * lax.axis_size("dev")), "dev", 0, 0), axis=0
+    )
     height = block_rows(gathered.shape[0])
     block_count = gathered.shape[0] // height
     blocks = gathered.reshape(block_count, height, gathered.shape[1])

time: 528 us -> 513 us (0.972)
  blocking collectives: 128 us -> 74.5 us
  waiting for transfers between devices: 182 us -> 208 us
  starting transfers between devices: 0.04 us -> 11.7 us
    all_gather x1 -> x0, blocking collectives: 53.8 us -> none  [local(): gathered = lax.all_gather(references, 'dev', axis=0, tiled=True)]
    all_to_all x0 -> x1, waiting for transfers between devices: none -> 26.3 us  [local(): lax.all_to_all(jnp.stack([references] * lax.axis_size('dev')), 'dev', 0, 0)]
    all_to_all x0 -> x1, starting transfers between devices: none -> 11.6 us  [local(): lax.all_to_all(jnp.stack([references] * lax.axis_size('dev')), 'dev', 0, 0)]
  transfers between devices with their start and end apart: 1 -> 2, of which waited for: 1 -> 2; matrix products, arithmetic and copies ran while one was open for 0% -> 0% of each run, Pallas kernels for 0% -> 0%
where the time goes in v1:
time: 513 us; the launch traced here: 511 us
  waiting for transfers between devices  208 us (41%)
  matrix products  81.5 us (16%)
  blocking collectives  74.5 us (15%)
  local copies, waits for them, and re-layouts  66.7 us (13%)
  other arithmetic  42.8 us (8%)
  between operations  14.2 us (3%)
  loops' own time  12.1 us (2%)
  starting transfers between devices  11.7 us (2%)
    psum x1, waiting for transfers between devices, local(): merged = lax.psum((numer_all, cycles_all, mass_all), ('grp', 'dev'))  181 us
    psum x1, blocking collectives, local(): merged = lax.psum((numer_all, cycles_all, mass_all), ('grp', 'dev'))  74.5 us
    dot_general x16, matrix products, block_scores(): jnp.einsum('pkmc,mcb->pmkb', stacked, weighted, preferred_element_type=jn...  32.7 us
    all_to_all x1, waiting for transfers between devices, local(): lax.all_to_all(jnp.stack([references] * lax.axis_size('dev')), 'dev', 0, 0)  26.3 us
    dot_general x16, matrix products, block_scores(): jnp.einsum('pmkb,pmr->krb', crossed, score_table, preferred_element_type=...  26.3 us
    dynamic_slice x32, local copies, waits for them, and re-layouts, local(): lax.scan(one_block, initial, (blocks, jnp.arange(block_count, dtype=jnp.i...  23.9 us
    reduce_sum x16, other arithmetic, class_rows(): jnp.sum(squares, axis=2) * factor[None, :, None]  18.6 us
    dot_general x8, matrix products, one_block(): jnp.einsum('pmkb,mcb->kpmc', spectra, weighted, preferred_element_type=jn...  15.7 us
  transfers between devices with their start and end apart: 2, of which 2 were waited for; matrix products, arithmetic and copies ran while one was open for 0% of the time, Pallas kernels for 0%

profile of v1, /device:TPU:2, one launch (start us, length us, event | category | flops | bytes accessed | tf_op | source)
XLA Modules:
  0.0 510.9 jit_solution(3489984348825701169)
XLA Ops:
  7.2 2.0 stack.22
  9.2 11.6 %all-to-all-start = ((bf16[32,6,2048]{2,1,0:T(8,128)(2,1)}), bf16[32,6,2048]{2,1,0:T(8,128)(2,1)S(1)}, u32[]{:S(2)}, u32[]{:S(2)}) async-start(bf16[32,6,2048]{2,1,0:T(8,128)(2,1)} %stack.22), calls=%async_computation | async-start | bytes 2097152 | tf_op jit(solution)/shard_map/all_to_all | solution.py:86
  22.6 26.3 %all-to-all-done = bf16[32,6,2048]{2,1,0:T(8,128)(2,1)S(1)} async-done(((bf16[32,6,2048]{2,1,0:T(8,128)(2,1)}), bf16[32,6,2048]{2,1,0:T(8,128)(2,1)S(1)}, u32[]{:S(2)}, u32[]{:S(2)}) %all-to-all-start) | async-done | bytes 786464 | tf_op jit(solution)/shard_map/all_to_all | solution.py:86
  50.1 87.8 %while.28 = (s32[]{:T(128)}, f32[256]{0:T(256)S(1)}, f32[256]{0:T(256)S(1)}, bf16[8,24,2048]{2,1,0:T(8,128)(2,1)}, bf16[32,64,256]{2,1,0:T(8,128)(2,1)}, /*index...) while((s32[]{:T(128)}, f32[256]{0:T(256)S(1)}, ...), condition=%wide.region_5.6_spmd.clone, body=%wide.region_0.5_spmd.clone.sunk | while | flops 159947328 | bytes 10727242 | solution.py:100
  52.9 2.5 fusion.111
  58.1 2.0 fusion.112
  63.9 2.5 fusion.111
  69.1 2.0 fusion.112
  74.8 2.5 fusion.111
  80.1 2.0 fusion.112
  85.8 2.5 fusion.111
  91.1 2.0 fusion.112
  96.8 2.5 fusion.111
  102.1 2.0 fusion.112
  107.8 2.5 fusion.111
  113.0 2.0 fusion.112
  118.8 2.5 fusion.111
  124.0 2.0 fusion.112
  129.8 2.5 fusion.111
  135.0 2.0 fusion.112
  138.2 106.6 %while.27 = (s32[]{:T(128)}, f32[192,2048]{1,0:T(8,128)S(1)}, f32[192,32]{1,0:T(8,128)S(1)}, f32[192]{0:T(256)S(1)}, bf16[8,24,2048]{2,1,0:T(8,128)(2,1)}, /*ind...) while((s32[]{:T(128)}, f32[192,2048]{1,0:T(8,128)S(1)}, ...), condition=%wide.region_11.12_spmd, body=%wide.region_6.11_spmd.sunk | while | flops 313785664 | bytes 12832803 | solution.py:132
  160.5 2.0 convolution_bitcast_fusion.3
  246.0 74.5 %all-reduce = (f32[192,32]{1,0:T(8,128)S(1)}, f32[192]{0:T(256)S(1)}) all-reduce(f32[192,32]{1,0:T(8,128)S(1)} %get-tuple-element.117, f32[192]{0:T(256)S(1)} %get-tuple-element.118), channel_id=1, replica_groups=mesh['grp'=8,'dev'=32] {'grp','dev'}, use_global_device_ids=true, to_apply=%region_13.14 | all-reduce | flops 6336 | bytes 50688 | tf_op jit(solution)/shard_map/psum | solution.py:136
  321.3 181.1 %all-reduce.3.cloned.1.call-done = f32[192,2048]{1,0:T(8,128)} async-done(((f32[192,2048]{1,0:T(8,128)}), f32[192,2048]{1,0:T(8,128)}) %all-reduce.3.cloned.1.call-update) | async-done | bytes 1572880 | tf_op jit(solution)/shard_map/psum | solution.py:136
  (355 shorter events, 151.1 us)
Async XLA Ops:
  7.2 14.0 %copy-start = (f32[64,32]{0,1:T(8,128)S(1)}, f32[64,32]{0,1:T(8,128)}, u32[]{:S(2)}) copy-start(f32[64,32]{0,1:T(8,128)} %param.13) | copy-start | bytes 24580
  7.2 14.0 %copy-start.3 = (s32[256]{0:T(256)S(1)}, s32[256]{0:T(256)}, u32[]{:S(2)}) copy-start(s32[256]{0:T(256)} %param.12) | copy-start | bytes 3076
  7.2 14.0 %copy-start.5 = (f32[32]{0:T(128)S(1)}, f32[32]{0:T(128)}, u32[]{:S(2)}) copy-start(f32[32]{0:T(128)} %param.14) | copy-start | bytes 388
  7.2 14.1 %copy-start.2 = (bf16[2048,256]{1,0:T(8,128)(2,1)S(1)}, bf16[2048,256]{1,0:T(8,128)(2,1)}, u32[]{:S(2)}) copy-start(bf16[2048,256]{1,0:T(8,128)(2,1)} %param.11) | copy-start | bytes 3145732
  9.2 40.9 %copy-start.4 = (f32[192]{0:T(256)S(1)}, f32[192]{0:T(256)}, u32[]{:S(2)}) copy-start(f32[192]{0:T(256)} %param.15) | copy-start | bytes 2308
  9.2 39.7 %all-to-all-start = ((bf16[32,6,2048]{2,1,0:T(8,128)(2,1)}), bf16[32,6,2048]{2,1,0:T(8,128)(2,1)S(1)}, u32[]{:S(2)}, u32[]{:S(2)}) async-start(bf16[32,6,2048]{2,1,0:T(8,128)(2,1)} %stack.22), calls=%async_computation | async-start | bytes 2097152 | tf_op jit(solution)/shard_map/all_to_all | solution.py:86
  20.8 481.7 %all-reduce.3.cloned.1.call-start = ((), (), s32[]{:S(2)}) async-start(), calls=%async_computation.1 | async-start | bytes 3145728 | tf_op jit(solution)/shard_map/psum | solution.py:136
  244.8 1.1 copy-start.1
Sparse Core Ops, SparseCore 0:
  246.1 256.3 all-reduce.2

commit v2 on v0

--- a/solution.py
+++ b/solution.py
@@ -131,7 +131,7 @@
         one_block, empty_sums, (blocks, jnp.arange(block_count, dtype=jnp.int32))
     )
     numer_all, cycles_all, mass_all = result
-    merged = lax.psum((numer_all, cycles_all, mass_all), ("grp", "dev"))
+    merged = lax.psum(lax.psum((numer_all, cycles_all, mass_all), "grp"), "dev")
     own_start = lax.axis_index("dev") * CLS_DEV
     numerator = lax.dynamic_slice_in_dim(merged[0], own_start, CLS_DEV, 0)
     cycle_sum = lax.dynamic_slice_in_dim(merged[1], own_start, CLS_DEV, 0)

time: 528 us -> 506 us (0.958)
  waiting for transfers between devices: 182 us -> 64.3 us
  blocking collectives: 128 us -> 222 us
    psum x1 -> x2, waiting for transfers between devices: 182 us -> 64.3 us  [local(): merged = lax.psum(lax.psum((numer_all, cycles_all, mass_all), 'grp'), 'dev')]
    psum x1 -> x2, blocking collectives: 73.8 us -> 168 us  [local(): merged = lax.psum(lax.psum((numer_all, cycles_all, mass_all), 'grp'), 'dev')]
  transfers between devices with their start and end apart: 1 -> 2, of which waited for: 1 -> 1; matrix products, arithmetic and copies ran while one was open for 0% -> 0% of each run, Pallas kernels for 0% -> 0%
where the time goes in v2:
time: 506 us; the launch traced here: 502 us
  blocking collectives  222 us (44%)
  matrix products  82.1 us (16%)
  local copies, waits for them, and re-layouts  64.6 us (13%)
  waiting for transfers between devices  64.3 us (13%)
  other arithmetic  42.8 us (8%)
  between operations  14.2 us (3%)
  loops' own time  12.1 us (2%)
    psum x2, blocking collectives, local(): merged = lax.psum(lax.psum((numer_all, cycles_all, mass_all), 'grp'), 'dev')  168 us
    psum x2, waiting for transfers between devices, local(): merged = lax.psum(lax.psum((numer_all, cycles_all, mass_all), 'grp'), 'dev')  64.3 us
    all_gather x1, blocking collectives, local(): gathered = lax.all_gather(references, 'dev', axis=0, tiled=True)  53.8 us
    dot_general x16, matrix products, block_scores(): jnp.einsum('pkmc,mcb->pmkb', stacked, weighted, preferred_element_type=jn...  32.7 us
    dot_general x16, matrix products, block_scores(): jnp.einsum('pmkb,pmr->krb', crossed, score_table, preferred_element_type=...  26.3 us
    dynamic_slice x32, local copies, waits for them, and re-layouts, local(): lax.scan(one_block, initial, (blocks, jnp.arange(block_count, dtype=jnp.i...  23.9 us
    reduce_sum x16, other arithmetic, class_rows(): jnp.sum(squares, axis=2) * factor[None, :, None]  18.6 us
    dot_general x8, matrix products, one_block(): jnp.einsum('pmkb,mcb->kpmc', spectra, weighted, preferred_element_type=jn...  15.7 us
  transfers between devices with their start and end apart: 2, of which 1 were waited for; matrix products, arithmetic and copies ran while one was open for 0% of the time, Pallas kernels for 0%

profile of v2, /device:TPU:2, one launch (start us, length us, event | category | flops | bytes accessed | tf_op | source)
XLA Modules:
  0.0 502.5 jit_solution(8308130179237923464)
XLA Ops:
  7.5 53.8 %all-gather = bf16[32,6,2048]{2,1,0:T(8,128)(2,1)S(1)} all-gather(bf16[1,6,2048]{2,1,0:T(8,128)(2,1)} %bitcast.179), channel_id=1, replica_groups=mesh['grp'=8,'dev'=32] {'dev'}, dimensions={0}, use_global_device_ids=true | all-gather | bytes 811008 | tf_op jit(solution)/shard_map/all_gather | solution.py:85
  64.5 87.8 %while.28 = (s32[]{:T(128)}, f32[256]{0:T(256)S(1)}, f32[256]{0:T(256)S(1)}, bf16[8,24,2048]{2,1,0:T(8,128)(2,1)}, bf16[32,64,256]{2,1,0:T(8,128)(2,1)}, /*index...) while((s32[]{:T(128)}, f32[256]{0:T(256)S(1)}, ...), condition=%wide.region_5.6_spmd.clone, body=%wide.region_0.5_spmd.clone.sunk | while | flops 159947328 | bytes 10727242 | solution.py:98
  67.3 2.5 fusion.111
  72.5 2.0 fusion.112
  78.3 2.5 fusion.111
  83.5 2.0 fusion.112
  89.2 2.5 fusion.111
  94.5 2.0 fusion.112
  100.2 2.5 fusion.111
  105.5 2.0 fusion.112
  111.2 2.5 fusion.111
  116.5 2.0 fusion.112
  122.2 2.5 fusion.111
  127.4 2.0 fusion.112
  133.2 2.5 fusion.111
  138.4 2.0 fusion.112
  144.2 2.5 fusion.111
  149.4 2.0 fusion.112
  152.6 106.6 %while.27 = (s32[]{:T(128)}, f32[192,2048]{1,0:T(8,128)S(1)}, f32[192,32]{1,0:T(8,128)S(1)}, f32[192]{0:T(256)S(1)}, bf16[8,24,2048]{2,1,0:T(8,128)(2,1)}, /*ind...) while((s32[]{:T(128)}, f32[192,2048]{1,0:T(8,128)S(1)}, ...), condition=%wide.region_11.12_spmd, body=%wide.region_6.11_spmd.sunk | while | flops 313785664 | bytes 12832803 | solution.py:130
  161.6 2.0 convolution_bitcast_fusion.3
  188.2 2.0 convolution_bitcast_fusion.3
  260.4 64.3 %all-reduce.5.cloned.1.call-done = f32[192,2048]{1,0:T(8,128)} async-done(((f32[192,2048]{1,0:T(8,128)}), f32[192,2048]{1,0:T(8,128)}) %all-reduce.5.cloned.1.call-update) | async-done | bytes 1572880 | tf_op jit(solution)/shard_map/psum | solution.py:134
  324.7 25.1 %all-reduce.1 = (f32[192,32]{1,0:T(8,128)S(1)}, f32[192]{0:T(256)S(1)}) all-reduce(f32[192,32]{1,0:T(8,128)S(1)} %get-tuple-element.117, f32[192]{0:T(256)S(1)} %get-tuple-element.118), channel_id=1, replica_groups=mesh['grp'=8,'dev'=32] {'grp'}, use_global_device_ids=true, to_apply=%region_14.15 | all-reduce | flops 6336 | bytes 50688 | tf_op jit(solution)/shard_map/psum | solution.py:134
  349.8 143.4 %all-reduce = (f32[192,32]{1,0:T(8,128)S(1)}, f32[192]{0:T(256)S(1)}) all-reduce(f32[192,32]{1,0:T(8,128)S(1)} %get-tuple-element.195, f32[192]{0:T(256)S(1)} %get-tuple-element.196), channel_id=1, replica_groups=mesh['grp'=8,'dev'=32] {'dev'}, use_global_device_ids=true, to_apply=%region_15.16 | all-reduce | flops 6336 | bytes 50688 | tf_op jit(solution)/shard_map/psum | solution.py:134
  (353 shorter events, 149.8 us)
Async XLA Ops:
  7.2 55.2 %copy-start = (f32[64,32]{0,1:T(8,128)S(1)}, f32[64,32]{0,1:T(8,128)}, u32[]{:S(2)}) copy-start(f32[64,32]{0,1:T(8,128)} %param.13) | copy-start | bytes 24580
  7.2 56.1 %copy-start.2 = (bf16[2048,256]{1,0:T(8,128)(2,1)S(1)}, bf16[2048,256]{1,0:T(8,128)(2,1)}, u32[]{:S(2)}) copy-start(bf16[2048,256]{1,0:T(8,128)(2,1)} %param.11) | copy-start | bytes 3145732
  7.2 57.3 %copy-start.3 = (f32[192]{0:T(256)S(1)}, f32[192]{0:T(256)}, u32[]{:S(2)}) copy-start(f32[192]{0:T(256)} %param.15) | copy-start | bytes 2308
  7.2 317.5 %all-reduce.5.cloned.1.call-start = ((), (), s32[]{:S(2)}) async-start(), calls=%async_computation | async-start | bytes 3145728 | tf_op jit(solution)/shard_map/psum | solution.py:134
  259.2 1.1 copy-start.1
  260.4 233.7 %all-reduce.7.cloned.1.call-start = ((), (), s32[]{:S(2)}) async-start(), calls=%async_computation.1 | async-start | bytes 3145728 | tf_op jit(solution)/shard_map/psum | solution.py:134
Sparse Core Ops, SparseCore 0:
  260.5 64.1 all-reduce.4
  328.1 153.2 all-reduce.6
